TPU v7x, 128 devices: a whole 4x4x4 slice. The times are simulated.
128 devices in a mesh: scan: 8 (over z, x_lo), det: 16 (over y, x_hi, core).
Axes of the slice: x: 4 (x_hi: 2, x_lo: 2; x = x_hi * 2 + x_lo), y: 4, z: 4, core: 2. Of those that a mesh axis runs over, the one named last changes fastest.
Arguments:
- frames: bfloat16 [16, 1024, 16384], P('det', 'scan'), may hold values from -6 to 6
- offsets: int32 [16384, 2], P(('scan', 'det')), may hold values from -32 to 32
- bright: int32 [16384], P(('scan', 'det')), may hold values from 0 to 1, as said below
- aberration: float32 [2], replicated, may hold values from 0.5 to 2
Outputs:
- tiles: float32 [16, 8, 160], P('det', 'scan')
Inputs may be any that keep to these rules, and one draw needn't show every extreme that they name: bright[k] is 1 exactly where (k // 128 - a)^2 + (k % 128 - b)^2 <= R^2 and 0 elsewhere, for one centre with whole a in 62 .. 66 and whole b in 62 .. 66, and one whole radius R in 40 .. 56, all ranges inclusive; so at least one pixel is 1.
All inputs are finite; a program needn't handle non-finite values.
Results may differ from a plain program's by a relative error of at most 0.0023.
Values may be sent and summed in bfloat16 or wider, within the bound.
No kernel may reach another device: no remote copies, remote signals or barrier semaphores. Data moves between devices by JAX's collectives and lax.ppermute only.
A program may use at most 128 MiB of HBM per device.

v0:
```python
import math
import jax
import jax.numpy as jnp
from jax import lax
from jax.sharding import PartitionSpec as P

SR = 16
SC = 1024
DROWS = 128
DCOLS = 128
HALO = 16
TWO_PI = 2.0 * math.pi
EXACT_PRECISION = lax.Precision.HIGHEST


def phase_angles(first, second_operand, modulus):
    product = jnp.mod(first[:, None] * second_operand[None, :], modulus)
    return TWO_PI / modulus * product.astype(jnp.float32)


def signed_frequency(length):
    position = jnp.arange(length, dtype=jnp.int32)
    folded = jnp.where(position < length // 2, position, position - length)
    return 2.0 * folded.astype(jnp.float32) / length


def pixel_phase(pixel_index, shifts, aberration):
    freq_rows = signed_frequency(SR)[:, None, None]
    freq_cols = signed_frequency(SC)[None, :, None]
    half_rows = DROWS // 2
    half_cols = DCOLS // 2
    tilt_x = ((pixel_index // DCOLS - half_rows).astype(jnp.float32) / half_rows)[None, None, :]
    tilt_y = ((pixel_index % DCOLS - half_cols).astype(jnp.float32) / half_cols)[None, None, :]
    ramp_rows = jnp.mod(jnp.arange(SR, dtype=jnp.int32)[:, None] * shifts[:, 0][None, :], SR)
    ramp_cols = jnp.mod(jnp.arange(SC, dtype=jnp.int32)[:, None] * shifts[:, 1][None, :], SC)
    shift_phase = (
        TWO_PI / SR * ramp_rows.astype(jnp.float32)[:, None, :]
        + TWO_PI / SC * ramp_cols.astype(jnp.float32)[None, :, :]
    )
    tilt_sq = tilt_x * tilt_x + tilt_y * tilt_y
    tilt_dot = tilt_x * freq_rows + tilt_y * freq_cols
    moved_x = freq_rows + tilt_x
    moved_y = freq_cols + tilt_y
    moved_sq = moved_x * moved_x + moved_y * moved_y
    lens_phase = math.pi * (
        aberration[0] * (freq_rows * freq_rows + freq_cols * freq_cols)
        + aberration[1] * (moved_sq * moved_sq - tilt_sq * tilt_sq - 4.0 * tilt_sq * tilt_dot)
    )
    return shift_phase - lens_phase


def window_weights(width):
    position = jnp.arange(width, dtype=jnp.int32)
    nearest = jnp.minimum(position, width - 1 - position)
    ramped = 0.3 + 0.35 * (
        1.0 - jnp.cos(math.pi * (nearest.astype(jnp.float32) + 0.5) / (2 * HALO))
    )
    return jnp.where(nearest < 2 * HALO, ramped, jnp.float32(1.0))


def inverse_transform(spec_real, spec_imag, columns, rows):
    col_angles = phase_angles(jnp.arange(SC, dtype=jnp.int32), columns, SC)
    cos_cols = jnp.cos(col_angles)
    sin_cols = jnp.sin(col_angles)
    real_piece = jnp.dot(spec_real, cos_cols, precision=EXACT_PRECISION) - jnp.dot(
        spec_imag, sin_cols, precision=EXACT_PRECISION
    )
    imaginary_piece = jnp.dot(spec_real, sin_cols, precision=EXACT_PRECISION) + jnp.dot(
        spec_imag, cos_cols, precision=EXACT_PRECISION
    )
    angles_by_row = phase_angles(jnp.arange(SR, dtype=jnp.int32), rows, SR)
    row_cosines = jnp.cos(angles_by_row)
    row_sines = jnp.sin(angles_by_row)
    return jnp.dot(row_cosines.T, real_piece, precision=EXACT_PRECISION) - jnp.dot(
        row_sines.T, imaginary_piece, precision=EXACT_PRECISION
    )


def local(frames, offsets, bright, aberration):
    scan_size = lax.axis_size("scan")
    det_size = lax.axis_size("det")
    rows_dev, tile, detector = frames.shape
    owned = offsets.shape[0]
    groups = detector // owned
    owner = lax.axis_index("scan") * det_size + lax.axis_index("det")
    blocks = jnp.transpose(frames.reshape(rows_dev * tile, groups, owned), (1, 0, 2))
    arrived = lax.all_to_all(blocks, ("scan", "det"), split_axis=0, concat_axis=0, tiled=True)
    images = arrived.reshape(scan_size, det_size, rows_dev, tile, owned)
    full_cols = jnp.arange(SC, dtype=jnp.int32)
    col_angles = phase_angles(full_cols, full_cols, SC)
    col_cos = jnp.cos(col_angles).astype(jnp.bfloat16)
    col_sin = jnp.sin(col_angles).astype(jnp.bfloat16)
    table = jnp.concatenate([col_cos, -col_sin], axis=1).reshape(scan_size, tile, 2 * SC)
    both_col = jnp.einsum(
        "abrcp,acq->brqp", images, table, preferred_element_type=jnp.float32
    ).reshape(SR, 2 * SC, owned)
    real_col = both_col[:, :SC]
    imag_col = both_col[:, SC:]
    full_rows = jnp.arange(SR, dtype=jnp.int32)
    angles_by_row = phase_angles(full_rows, full_rows, SR)
    row_cos = jnp.cos(angles_by_row)
    row_sin = jnp.sin(angles_by_row)
    real_full = jnp.einsum(
        "rs,rqp->sqp", row_cos, real_col, precision=EXACT_PRECISION
    ) + jnp.einsum("rs,rqp->sqp", row_sin, imag_col, precision=EXACT_PRECISION)
    imag_full = jnp.einsum(
        "rs,rqp->sqp", row_cos, imag_col, precision=EXACT_PRECISION
    ) - jnp.einsum("rs,rqp->sqp", row_sin, real_col, precision=EXACT_PRECISION)
    pixel_index = owner * owned + jnp.arange(owned, dtype=jnp.int32)
    phase = pixel_phase(pixel_index, offsets, aberration)
    weights = bright.astype(jnp.float32)
    turn_cos = jnp.cos(phase) * weights
    turn_sin = jnp.sin(phase) * weights
    spec_real = jnp.sum(real_full * turn_cos - imag_full * turn_sin, axis=2)
    spec_imag = jnp.sum(real_full * turn_sin + imag_full * turn_cos, axis=2)
    packed = jnp.concatenate(
        [spec_real.reshape(-1), spec_imag.reshape(-1), jnp.sum(weights).reshape(1)]
    )
    total = lax.psum(packed, ("scan", "det"))
    spec_real = total[: SR * SC].reshape(SR, SC)
    spec_imag = total[SR * SC : 2 * SR * SC].reshape(SR, SC)
    bright_sum = total[2 * SR * SC]
    width = tile + 2 * HALO
    columns = jnp.mod(lax.axis_index("scan") * tile - HALO + jnp.arange(width, dtype=jnp.int32), SC)
    rows = lax.axis_index("det") * rows_dev + jnp.arange(rows_dev, dtype=jnp.int32)
    picture = inverse_transform(spec_real, spec_imag, columns, rows)
    return (
        picture * (1.0 / (SR * SC)) / jnp.sqrt(bright_sum) * window_weights(width)[None, :]
    ).reshape(rows_dev, 1, width)


def solution(mesh):
    placed = (P("det", "scan", None), P(("scan", "det"), None), P(("scan", "det")), P())
    return jax.shard_map(
        local, mesh=mesh, in_specs=placed, out_specs=P("det", "scan", None), check_vma=False
    )
```

profile of v0, /device:TPU:1, one launch (start us, length us, event | category | flops | bytes accessed | tf_op | source)
XLA Modules:
  0.0 367.1 jit_solution(14988252802277870520)
XLA Ops:
  6.5 6.4 %copy.37 = bf16[1,128,16384]{1,2,0:T(8,128)(2,1)} copy(bf16[1,128,16384]{2,1,0:T(8,128)(2,1)} %param.4) | data formatting | bytes 8388608 | tf_op args[0]
  12.9 11.9 %all-to-all-start = ((bf16[128,128,128]{1,2,0:T(8,128)(2,1)}), bf16[128,128,128]{1,2,0:T(8,128)(2,1)}, u32[]{:S(2)}, u32[]{:S(2)}) async-start(bf16[128,128,128]{1,2,0:T(8,128)(2,1)} %bitcast.61), calls=%async_computation | async-start | bytes 8388608 | tf_op jit(solution)/shard_map/all_to_all | solution.py:87
  24.9 0.0 all-reduce.2.cloned.1.call-start
  25.0 0.7 fusion.126
  25.7 0.7 add_multiply_fusion.1
  26.4 0.2 copy.42
  26.7 0.6 convert_reduce_fusion
  27.3 0.1 add_multiply_fusion.2
  27.4 0.3 fusion.27
  27.6 1.2 add_multiply_fusion
  28.9 15.5 %cosine_convert_fusion = bf16[8,128,1024]{1,2,0:T(8,128)(2,1)S(1)} fusion(s32[8,128]{1,0:T(8,128)S(1)} %multiply_add_fusion), kind=kLoop, calls=%fused_computation.25 | loop fusion | flops 15728640 | bytes 2101248 | tf_op jit(solution)/shard_map/convert_element_type | solution.py:91
  44.3 16.9 %fusion.18 = bf16[8,128,1024]{1,2,0:T(8,128)(2,1)} fusion(s32[8,128]{1,0:T(8,128)S(1)} %multiply_add_fusion), kind=kLoop, calls=%fused_computation.29 | loop fusion | flops 18874368 | bytes 2101248 | tf_op jit(solution)/shard_map/neg | solution.py:93
  61.2 15.5 %all-to-all-done = bf16[128,128,128]{1,2,0:T(8,128)(2,1)} async-done(((bf16[128,128,128]{1,2,0:T(8,128)(2,1)}), bf16[128,128,128]{1,2,0:T(8,128)(2,1)}, u32[]{:S(2)}, u32[]{:S(2)}) %all-to-all-start) | async-done | bytes 4194336 | tf_op jit(solution)/shard_map/all_to_all | solution.py:87
  76.8 13.4 %convolution_bitcast_fusion = f32[16,2048,128]{2,1,0:T(8,128)} fusion(bf16[8,16,128,128]{2,3,1,0:T(8,128)(2,1)} %bitcast.5, bf16[8,128,1024]{1,2,0:T(8,128)(2,1)} %fusion.18, bf16[8,128,1024]{1,2,0:T(8,128)(2,1)S(1)} %cosine_convert_fusion), kind=kOutput, calls=%fused_computation.13 | convolution fusion | flops 8598323200 | bytes 25165824 | tf_op jit(solution)/shard_map/abrcp,acq->brqp/dot_general | solution.py:94
  90.2 6.9 %fusion.124 = (f32[16,1024,128]{2,1,0:T(8,128)S(1)}, f32[16,1024,128]{2,1,0:T(8,128)S(1)}) fusion(f32[16,2048,128]{2,1,0:T(8,128)} %convolution_bitcast_fusion), kind=kLoop, calls=%fused_computation.169 | loop fusion | bytes 33554432 | tf_op jit(solution)/shard_map/slice | solution.py:97
  97.1 11.6 %fusion.4 = f32[16,1024,128]{2,0,1:T(8,128)S(1)} fusion(f32[16,1024,128]{2,1,0:T(8,128)S(1)} %get-tuple-element.7), kind=kOutput, calls=%fused_computation.9 | convolution fusion | flops 402656768 | bytes 16777216 | tf_op jit(solution)/shard_map/rs,rqp->sqp/dot_general | solution.py:108
  108.7 16.6 %fusion.6 = f32[16,1024,128]{2,0,1:T(8,128)} fusion(f32[16,1024,128]{2,1,0:T(8,128)S(1)} %get-tuple-element.7), kind=kOutput, calls=%fused_computation.11 | convolution fusion | flops 402656768 | bytes 16777216 | tf_op jit(solution)/shard_map/rs,rqp->sqp/dot_general | solution.py:103
  125.3 16.6 %fusion.2 = f32[16,1024,128]{2,0,1:T(8,128)} fusion(f32[16,1024,128]{2,1,0:T(8,128)S(1)} %get-tuple-element.8), kind=kOutput, calls=%fused_computation.7 | convolution fusion | flops 402656768 | bytes 16777216 | tf_op jit(solution)/shard_map/rs,rqp->sqp/dot_general | solution.py:105
  142.0 54.1 %subtract_reduce_fusion = (f32[16,1024]{0,1:T(8,128)S(1)}, f32[16,1024]{0,1:T(8,128)S(1)}) fusion(f32[128]{0:T(128)S(1)} %convert_element_type.122, f32[1024,128]{1,0:T(8,128)S(1)} %copy-done.2, f32[16,128]{1,0:T(8,128)S(1)} %get-tuple-element.16, f32[128]{0:T(128)S(1)} %get-tuple-element.21, f32[128]{0:T(128)S(1)} %get-tuple-element.22, ...), kind=kOutput, calls=%fused_computation.1 | convolution fusion | flops 450858496 | bytes 35350020 | tf_op jit(solution)/shard_map/rs,rqp->sqp/dot_general | solution.py:106
  196.1 0.2 copy.46
  196.3 0.2 copy.45
  196.5 1.3 pad_maximum_fusion
  197.8 140.7 %all-reduce.2.cloned.1.call-done = f32[32769]{0:T(1024)} async-done(((f32[32769]{0:T(1024)}), f32[32769]{0:T(1024)}) %all-reduce.2.cloned.1.call-update) | async-done | bytes 131092 | tf_op jit(solution)/shard_map/psum | solution.py:119
  338.5 0.9 fusion.125
  339.4 4.3 %fusion.31 = f32[16,160]{1,0:T(8,128)S(1)} fusion(f32[16,1024]{1,0:T(8,128)S(1)} %reshape.408, s32[160]{0:T(256)S(1)} %and_select_fusion), kind=kOutput, calls=%fused_computation.49 | convolution fusion | flops 33751040 | bytes 76416 | tf_op jit(solution)/shard_map/dot_general | solution.py:65
  343.8 4.4 %fusion.33 = f32[16,160]{1,0:T(8,128)S(1)} fusion(f32[16,1024]{1,0:T(8,128)S(1)} %reshape.408, s32[160]{0:T(256)S(1)} %and_select_fusion), kind=kOutput, calls=%fused_computation.50 | convolution fusion | flops 33751040 | bytes 76416 | tf_op jit(solution)/shard_map/dot_general | solution.py:68
  348.2 4.6 %convolution_subtract_fusion = f32[16,160]{1,0:T(8,128)S(1)} fusion(f32[16,160]{1,0:T(8,128)S(1)} %fusion.31, f32[16,1024]{1,0:T(8,128)S(1)} %reshape.409, s32[160]{0:T(256)S(1)} %and_select_fusion), kind=kOutput, calls=%fused_computation.34 | convolution fusion | flops 33753600 | bytes 86656 | tf_op jit(solution)/shard_map/dot_general | solution.py:65
  352.8 0.2 fusion.75
  353.0 4.4 %convolution_add_fusion = f32[16,160]{1,0:T(8,128)S(1)} fusion(f32[16,160]{1,0:T(8,128)S(1)} %fusion.33, f32[16,1024]{1,0:T(8,128)S(1)} %reshape.409, s32[160]{0:T(256)S(1)} %and_select_fusion), kind=kOutput, calls=%fused_computation.33 | convolution fusion | flops 33753600 | bytes 86656 | tf_op jit(solution)/shard_map/dot_general | solution.py:68
  357.3 0.2 fusion.73
  357.5 1.2 slice.40
  359.4 0.6 divide_multiply_fusion
  (28 shorter events, 0.2 us)
Async XLA Ops:
  6.5 18.4 %copy-start.5 = (s32[128]{0:T(128)S(1)}, s32[128]{0:T(128)}, u32[]{:S(2)}) copy-start(s32[128]{0:T(128)} %param.6) | copy-start | bytes 1540
  6.5 18.5 %copy-start.3 = (f32[2]{0:T(128)S(1)}, f32[2]{0:T(128)}, u32[]{:S(2)}) copy-start(f32[2]{0:T(128)} %param.7) | copy-start | bytes 28
  6.5 20.7 %copy-start.4 = (s32[128,2]{0,1:T(2,128)S(1)}, s32[128,2]{0,1:T(2,128)}, u32[]{:S(2)}) copy-start(s32[128,2]{0,1:T(2,128)} %param.5) | copy-start | bytes 3076
  12.9 63.8 %all-to-all-start = ((bf16[128,128,128]{1,2,0:T(8,128)(2,1)}), bf16[128,128,128]{1,2,0:T(8,128)(2,1)}, u32[]{:S(2)}, u32[]{:S(2)}) async-start(bf16[128,128,128]{1,2,0:T(8,128)(2,1)} %bitcast.61), calls=%async_computation | async-start | bytes 8388608 | tf_op jit(solution)/shard_map/all_to_all | solution.py:87
  24.9 313.6 %all-reduce.2.cloned.1.call-start = ((), (), s32[]{:S(2)}) async-start(), calls=%async_computation.1 | async-start | bytes 270336 | tf_op jit(solution)/shard_map/psum | solution.py:119
  125.3 16.7 %copy-start = (f32[16,1024,128]{2,0,1:T(8,128)S(1)}, f32[16,1024,128]{2,0,1:T(8,128)}, u32[]{:S(2)}) copy-start(f32[16,1024,128]{2,0,1:T(8,128)} %fusion.6) | copy-start | bytes 25165828
  125.3 16.7 %copy-start.1 = (f32[1024,128]{1,0:T(8,128)S(1)}, f32[1024,128]{1,0:T(8,128)}, u32[]{:S(2)}) copy-start(f32[1024,128]{1,0:T(8,128)} %get-tuple-element.11) | copy-start | bytes 1572868
  125.3 16.7 %copy-start.2 = (f32[1024,128]{1,0:T(8,128)S(1)}, f32[1024,128]{1,0:T(8,128)}, u32[]{:S(2)}) copy-start(f32[1024,128]{1,0:T(8,128)} %get-tuple-element.12) | copy-start | bytes 1572868
Sparse Core Ops, SparseCore 0:
  197.9 140.5 all-reduce.1
where the time goes:
time: 373 us; the launch traced here: 367 us
  waiting for transfers between devices  156 us (42%)
  matrix products  130 us (35%)
  other arithmetic  37.3 us (10%)
  local copies, waits for them, and re-layouts  16.7 us (4%)
  between operations  14.5 us (4%)
  starting transfers between devices  12 us (3%)
    psum x1, waiting for transfers between devices, local(): total = lax.psum(packed, ('scan', 'det'))  141 us
    dot_general x1, matrix products, local(): jnp.einsum('rs,rqp->sqp', row_cos, imag_col, precision=EXACT_PRECISION)  54.1 us
    neg x1, other arithmetic, local(): -col_sin  16.9 us
    dot_general x1, matrix products, local(): jnp.einsum('rs,rqp->sqp', row_sin, imag_col, precision=EXACT_PRECISION)  16.6 us
    dot_general x1, matrix products, local(): jnp.einsum('rs,rqp->sqp', row_cos, real_col, precision=EXACT_PRECISION)  16.6 us
    all_to_all x1, waiting for transfers between devices, local(): lax.all_to_all(blocks, ('scan', 'det'), split_axis=0, concat_axis=0, tile...  15.5 us
    convert_element_type x1, other arithmetic, local(): col_cos = jnp.cos(col_angles).astype(jnp.bfloat16)  15.5 us
    dot_general x1, matrix products, local(): jnp.einsum('abrcp,acq->brqp', images, table, preferred_element_type=jnp.f...  13.4 us
  transfers between devices with their start and end apart: 2, of which 2 were waited for; matrix products, arithmetic and copies ran while one was open for 10% of the time, Pallas kernels for 0%

commit v1 on v0

--- a/solution.py
+++ b/solution.py
@@ -116,7 +116,7 @@
     packed = jnp.concatenate(
         [spec_real.reshape(-1), spec_imag.reshape(-1), jnp.sum(weights).reshape(1)]
     )
-    total = lax.psum(packed, ("scan", "det"))
+    total = jnp.sum(lax.all_gather(packed, ("scan", "det")), axis=0)
     spec_real = total[: SR * SC].reshape(SR, SC)
     spec_imag = total[SR * SC : 2 * SR * SC].reshape(SR, SC)
     bright_sum = total[2 * SR * SC]

time: 373 us -> 483 us (1.29)
  waiting for transfers between devices: 156 us -> 230 us
  local copies, waits for them, and re-layouts: 16.7 us -> 44.5 us
  other arithmetic: 37.3 us -> 45.2 us
    unnamed x1 -> x2, waiting for transfers between devices: 0.02 us -> 215 us
    psum x1 -> x0, waiting for transfers between devices: 141 us -> none  [local(): total = lax.psum(packed, ('scan', 'det'))]
    all_gather x0 -> x1, local copies, waits for them, and re-layouts: none -> 23 us  [local(): total = jnp.sum(lax.all_gather(packed, ('scan', 'det')), axis=0)]
    reduce_sum x0 -> x1, other arithmetic: none -> 6.91 us  [local(): total = jnp.sum(lax.all_gather(packed, ('scan', 'det')), axis=0)]
    unnamed x15 -> x16, local copies, waits for them, and re-layouts: 6.47 us -> 12.8 us
  transfers between devices with their start and end apart: 2 -> 2, of which waited for: 2 -> 2; matrix products, arithmetic and copies ran while one was open for 10% -> 8% of each run, Pallas kernels for 0% -> 0%
where the time goes in v1:
time: 483 us; the launch traced here: 477 us
  waiting for transfers between devices  230 us (48%)
  matrix products  130 us (27%)
  other arithmetic  45.2 us (9%)
  local copies, waits for them, and re-layouts  44.5 us (9%)
  between operations  14.5 us (3%)
  starting transfers between devices  12 us (2%)
    unnamed x2, waiting for transfers between devices  215 us
    dot_general x1, matrix products, local(): jnp.einsum('rs,rqp->sqp', row_cos, imag_col, precision=EXACT_PRECISION)  53.6 us
    all_gather x1, local copies, waits for them, and re-layouts, local(): total = jnp.sum(lax.all_gather(packed, ('scan', 'det')), axis=0)  23 us
    neg x1, other arithmetic, local(): -col_sin  16.9 us
    dot_general x1, matrix products, local(): jnp.einsum('rs,rqp->sqp', row_cos, real_col, precision=EXACT_PRECISION)  16.9 us
    dot_general x1, matrix products, local(): jnp.einsum('rs,rqp->sqp', row_sin, imag_col, precision=EXACT_PRECISION)  16.6 us
    all_to_all x1, waiting for transfers between devices, local(): lax.all_to_all(blocks, ('scan', 'det'), split_axis=0, concat_axis=0, tile...  15.6 us
    convert_element_type x1, other arithmetic, local(): col_cos = jnp.cos(col_angles).astype(jnp.bfloat16)  15.5 us
  transfers between devices with their start and end apart: 2, of which 2 were waited for; matrix products, arithmetic and copies ran while one was open for 8% of the time, Pallas kernels for 0%

profile of v1, /device:TPU:1, one launch (start us, length us, event | category | flops | bytes accessed | tf_op | source)
XLA Modules:
  0.0 476.6 jit_solution(13541907222228300658)
XLA Ops:
  6.5 6.4 %copy.37 = bf16[1,128,16384]{1,2,0:T(8,128)(2,1)} copy(bf16[1,128,16384]{2,1,0:T(8,128)(2,1)} %param.4) | data formatting | bytes 8388608 | tf_op args[0]
  12.9 11.9 %all-to-all-start = ((bf16[128,128,128]{1,2,0:T(8,128)(2,1)}), bf16[128,128,128]{1,2,0:T(8,128)(2,1)}, u32[]{:S(2)}, u32[]{:S(2)}) async-start(bf16[128,128,128]{1,2,0:T(8,128)(2,1)} %bitcast.61), calls=%async_computation | async-start | bytes 8388608 | tf_op jit(solution)/shard_map/all_to_all | solution.py:87
  25.0 0.6 fusion.126
  25.6 0.7 add_multiply_fusion.1
  26.3 0.2 copy.42
  26.6 0.6 convert_reduce_fusion
  27.3 0.3 fusion.27
  27.6 1.2 add_multiply_fusion
  28.8 15.5 %cosine_convert_fusion = bf16[8,128,1024]{1,2,0:T(8,128)(2,1)S(1)} fusion(s32[8,128]{1,0:T(8,128)S(1)} %multiply_add_fusion), kind=kLoop, calls=%fused_computation.25 | loop fusion | flops 15728640 | bytes 2101248 | tf_op jit(solution)/shard_map/convert_element_type | solution.py:91
  44.3 16.9 %fusion.18 = bf16[8,128,1024]{1,2,0:T(8,128)(2,1)} fusion(s32[8,128]{1,0:T(8,128)S(1)} %multiply_add_fusion), kind=kLoop, calls=%fused_computation.29 | loop fusion | flops 18874368 | bytes 2101248 | tf_op jit(solution)/shard_map/neg | solution.py:93
  61.2 15.6 %all-to-all-done = bf16[128,128,128]{1,2,0:T(8,128)(2,1)} async-done(((bf16[128,128,128]{1,2,0:T(8,128)(2,1)}), bf16[128,128,128]{1,2,0:T(8,128)(2,1)}, u32[]{:S(2)}, u32[]{:S(2)}) %all-to-all-start) | async-done | bytes 4194336 | tf_op jit(solution)/shard_map/all_to_all | solution.py:87
  76.8 13.5 %convolution_bitcast_fusion = f32[16,2048,128]{2,1,0:T(8,128)} fusion(bf16[8,16,128,128]{2,3,1,0:T(8,128)(2,1)} %bitcast.5, bf16[8,128,1024]{1,2,0:T(8,128)(2,1)} %fusion.18, bf16[8,128,1024]{1,2,0:T(8,128)(2,1)S(1)} %cosine_convert_fusion), kind=kOutput, calls=%fused_computation.13 | convolution fusion | flops 8598323200 | bytes 25165824 | tf_op jit(solution)/shard_map/abrcp,acq->brqp/dot_general | solution.py:94
  90.2 7.0 %fusion.124 = (f32[16,1024,128]{2,1,0:T(8,128)S(1)}, f32[16,1024,128]{2,1,0:T(8,128)S(1)}) fusion(f32[16,2048,128]{2,1,0:T(8,128)} %convolution_bitcast_fusion), kind=kLoop, calls=%fused_computation.169 | loop fusion | bytes 33554432 | tf_op jit(solution)/shard_map/slice | solution.py:97
  97.3 11.6 %fusion.4 = f32[16,1024,128]{2,0,1:T(8,128)S(1)} fusion(f32[16,1024,128]{2,1,0:T(8,128)S(1)} %get-tuple-element.7), kind=kOutput, calls=%fused_computation.9 | convolution fusion | flops 402656768 | bytes 16777216 | tf_op jit(solution)/shard_map/rs,rqp->sqp/dot_general | solution.py:108
  108.9 16.9 %fusion.6 = f32[16,1024,128]{2,0,1:T(8,128)} fusion(f32[16,1024,128]{2,1,0:T(8,128)S(1)} %get-tuple-element.7), kind=kOutput, calls=%fused_computation.11 | convolution fusion | flops 402656768 | bytes 16777216 | tf_op jit(solution)/shard_map/rs,rqp->sqp/dot_general | solution.py:103
  125.8 16.6 %fusion.2 = f32[16,1024,128]{2,0,1:T(8,128)} fusion(f32[16,1024,128]{2,1,0:T(8,128)S(1)} %get-tuple-element.8), kind=kOutput, calls=%fused_computation.7 | convolution fusion | flops 402656768 | bytes 16777216 | tf_op jit(solution)/shard_map/rs,rqp->sqp/dot_general | solution.py:105
  142.3 53.6 %subtract_reduce_fusion = (f32[16,1024]{0,1:T(8,128)S(1)}, f32[16,1024]{0,1:T(8,128)S(1)}) fusion(f32[128]{0:T(128)S(1)} %convert_element_type.122, f32[1024,128]{1,0:T(8,128)S(1)} %copy-done.2, f32[16,128]{1,0:T(8,128)S(1)} %get-tuple-element.16, f32[128]{0:T(128)S(1)} %get-tuple-element.21, f32[128]{0:T(128)S(1)} %get-tuple-element.22, ...), kind=kOutput, calls=%fused_computation.1 | convolution fusion | flops 450858496 | bytes 35350020 | tf_op jit(solution)/shard_map/rs,rqp->sqp/dot_general | solution.py:106
  196.0 0.2 copy.45
  196.2 0.2 copy.46
  196.4 6.3 %broadcast.581 = f32[4194432]{0:T(1024)} broadcast(f32[]{:T(128)} %constant.163.clone.1), dimensions={} | broadcast | bytes 16777732
  202.7 2.3 maximum_dynamic-update-slice_fusion
  205.1 214.6 %all-reduce.3.cloned.1.call-done = f32[4194432]{0:T(1024)} async-done(((f32[4194432]{0:T(1024)}), f32[4194432]{0:T(1024)}) %all-reduce.3.cloned.1.call-update) | async-done | bytes 16777744
  419.7 23.0 %reshape.411 = f32[128,32769]{1,0:T(8,128)} reshape(f32[4194432]{0:T(1024)} %all-reduce.3.cloned.1.call-done) | data formatting | bytes 33555456 | tf_op jit(solution)/shard_map/all_gather | solution.py:119
  442.7 6.9 %reduce_sum.39 = f32[32769]{0:T(1024)S(1)} reduce(f32[128,32769]{1,0:T(8,128)} %reshape.411, f32[]{:T(128)} %constant.163.clone.1), dimensions={0}, to_apply=%region_3.4 | reduce | flops 4161663 | bytes 16908808 | tf_op jit(solution)/shard_map/reduce_sum | solution.py:119
  449.6 0.5 slice.40
  450.2 4.4 fusion.33
  454.5 4.3 fusion.31
  459.6 4.6 convolution_subtract_fusion
  464.2 4.3 convolution_add_fusion
  468.5 0.2 fusion.73
  468.7 0.2 fusion.75
  468.9 0.6 divide_multiply_fusion
  (31 shorter events, 0.3 us)
Async XLA Ops:
  6.5 18.4 %copy-start.5 = (s32[128]{0:T(128)S(1)}, s32[128]{0:T(128)}, u32[]{:S(2)}) copy-start(s32[128]{0:T(128)} %param.6) | copy-start | bytes 1540
  6.5 18.5 %copy-start.3 = (f32[2]{0:T(128)S(1)}, f32[2]{0:T(128)}, u32[]{:S(2)}) copy-start(f32[2]{0:T(128)} %param.7) | copy-start | bytes 28
  6.5 20.7 %copy-start.4 = (s32[128,2]{0,1:T(2,128)S(1)}, s32[128,2]{0,1:T(2,128)}, u32[]{:S(2)}) copy-start(s32[128,2]{0,1:T(2,128)} %param.5) | copy-start | bytes 3076
  12.9 63.8 %all-to-all-start = ((bf16[128,128,128]{1,2,0:T(8,128)(2,1)}), bf16[128,128,128]{1,2,0:T(8,128)(2,1)}, u32[]{:S(2)}, u32[]{:S(2)}) async-start(bf16[128,128,128]{1,2,0:T(8,128)(2,1)} %bitcast.61), calls=%async_computation | async-start | bytes 8388608 | tf_op jit(solution)/shard_map/all_to_all | solution.py:87
  24.9 394.8 %all-reduce.3.cloned.1.call-start = ((), (), s32[]{:S(2)}) async-start(), calls=%async_computation.1 | async-start | bytes 33562624
  125.8 16.6 %copy-start = (f32[16,1024,128]{2,0,1:T(8,128)S(1)}, f32[16,1024,128]{2,0,1:T(8,128)}, u32[]{:S(2)}) copy-start(f32[16,1024,128]{2,0,1:T(8,128)} %fusion.6) | copy-start | bytes 25165828
  125.8 16.6 %copy-start.1 = (f32[1024,128]{1,0:T(8,128)S(1)}, f32[1024,128]{1,0:T(8,128)}, u32[]{:S(2)}) copy-start(f32[1024,128]{1,0:T(8,128)} %get-tuple-element.11) | copy-start | bytes 1572868
  125.8 16.6 %copy-start.2 = (f32[1024,128]{1,0:T(8,128)S(1)}, f32[1024,128]{1,0:T(8,128)}, u32[]{:S(2)}) copy-start(f32[1024,128]{1,0:T(8,128)} %get-tuple-element.12) | copy-start | bytes 1572868
Sparse Core Ops, SparseCore 0:
  205.2 214.4 all-reduce.2
